TPU v7x, 128 devices: a whole 4x4x4 slice. The times are simulated.
128 devices in a mesh: wa: 16 (over z, y_hi, core), an: 8 (over y_lo, x).
Axes of the slice: x: 4, y: 4 (y_hi: 2, y_lo: 2; y = y_hi * 2 + y_lo), z: 4, core: 2. Of those that a mesh axis runs over, the one named last changes fastest.
Arguments:
- mass_field: float32 [64, 256, 128, 256], P(None, 'wa', 'an'), may hold values from -8 to 8
- factor_one: float32 [256, 64], replicated, may hold values from -0.375 to 0.375
- factor_two: float32 [256, 64], P('wa'), may hold values from -0.375 to 0.375
- factor_four: float32 [64, 16], replicated, may hold values from -0.75 to 0.75
Outputs:
- gram: float32 [128, 128], P('an')
All inputs are finite; a program needn't handle non-finite values.
Results may differ from a plain program's by a relative error of at most 0.0001.
Values sent between devices are 32-bit elements; how exact they have to be, the bound alone decides.
No kernel may reach another device: no remote copies, remote signals or barrier semaphores. Data moves between devices by JAX's collectives and lax.ppermute only.
A program may use at most 128 MiB of HBM per device.

v0:
```python
import jax
import jax.numpy as jnp
from jax import lax
from jax.sharding import PartitionSpec as P


def on_device(mass_field, factor_one, factor_two, factor_four):
    highest = lax.Precision.HIGHEST
    species_count, fibre_cells, slab_cells, first_cells = mass_field.shape
    rank_one = factor_one.shape[1]
    rank_two = factor_two.shape[1]
    rank_four = factor_four.shape[1]
    reduced = jnp.dot(factor_four.T, mass_field.reshape(species_count, -1), precision=highest)
    reduced = reduced.reshape(rank_four * fibre_cells * slab_cells, first_cells)
    slab_rows = rank_one // lax.axis_size("wa")
    mixed_rows = jnp.dot(reduced, factor_one, precision=highest)
    mixed_rows = mixed_rows.reshape(rank_four, fibre_cells, slab_cells, rank_one)
    term = jnp.einsum("qjkr,jp->rkqp", mixed_rows, factor_two, precision=highest)
    summed = lax.psum(term.reshape(rank_one, slab_cells, rank_four * rank_two), "wa")
    owned_slab = lax.dynamic_slice_in_dim(summed, lax.axis_index("wa") * slab_rows, slab_rows, 0)
    partial_gram = jnp.einsum(
        "rim,rjm->ij",
        owned_slab,
        lax.all_gather(owned_slab, "an", axis=1, tiled=True),
        precision=highest,
    )
    gram_rows = lax.psum(partial_gram, "wa")
    return gram_rows / (rank_one * rank_two * rank_four)


def solution(mesh):
    in_specs = (P(None, "wa", "an", None), P(), P("wa", None), P())
    out_specs = P("an", None)
    return jax.shard_map(
        on_device, mesh=mesh, in_specs=in_specs, out_specs=out_specs, check_vma=False
    )
```

profile of v0, /device:TPU:1, one launch (start us, length us, event | category | flops | bytes accessed | tf_op | source)
XLA Modules:
  0.0 312.5 jit_solution(3219890865373004460)
XLA Ops:
  6.5 0.0 copy-start
  6.5 0.0 all-reduce.2.cloned.1.call-start
  6.5 22.7 %fusion = f32[16,16,16,256]{3,0,2,1:T(8,128)S(1)} fusion(f32[16,16,256,64]{2,1,0,3:T(8,128)} %bitcast.35, f32[64,16]{0,1:T(8,128)} %param.7), kind=kOutput, calls=%fused_computation | convolution fusion | flops 805306368 | bytes 20975616 | tf_op jit(solution)/shard_map/dot_general | solution.py:13
  29.3 0.0 copy-done
  29.3 0.0 copy-start.1
  29.3 5.6 %fusion.2 = f32[16,16,16,64]{3,1,2,0:T(8,128)S(1)} fusion(f32[16,16,16,256]{3,0,2,1:T(8,128)S(1)} %fusion, f32[256,64]{0,1:T(8,128)S(1)} %copy-done), kind=kOutput, calls=%fused_computation.2 | convolution fusion | flops 805306368 | bytes 5308416 | tf_op jit(solution)/shard_map/dot_general | solution.py:16
  34.9 0.0 copy-done.1
  34.9 13.5 %convolution_bitcast_fusion = f32[64,16,16,64]{3,0,1,2:T(8,128)S(1)} fusion(f32[16,16,16,64]{3,1,2,0:T(8,128)S(1)} %fusion.2, f32[16,64]{1,0:T(8,128)S(1)} %copy-done.1), kind=kOutput, calls=%fused_computation.4 | convolution fusion | flops 201326592 | bytes 5246976 | tf_op jit(solution)/shard_map/qjkr,jp->rkqp/dot_general | solution.py:18
  48.4 8.3 %copy.5 = f32[64,16,16,64]{3,2,1,0:T(8,128)} copy(f32[64,16,16,64]{3,0,1,2:T(8,128)S(1)} %convolution_bitcast_fusion) | data formatting | bytes 8388608 | tf_op jit(solution)/shard_map/qjkr,jp->rkqp/transpose | solution.py:18
  56.7 7.6 %reshape.12 = f32[64,16,1024]{2,1,0:T(8,128)} reshape(f32[64,16,16,64]{3,2,1,0:T(8,128)} %copy.5) | data formatting | bytes 8388608 | tf_op jit(solution)/shard_map/reshape | solution.py:19
  64.3 0.0 all-reduce.2.cloned.1.call-update
  64.4 0.0 all-gather.2.cloned.1.call-start
  64.4 158.7 %all-reduce.2.cloned.1.call-done = f32[64,16,1024]{2,1,0:T(8,128)} async-done(((f32[64,16,1024]{2,1,0:T(8,128)}), f32[64,16,1024]{2,1,0:T(8,128)}) %all-reduce.2.cloned.1.call-update) | async-done | bytes 4194320 | tf_op jit(solution)/shard_map/psum | solution.py:19
  223.1 1.7 constant_dynamic-slice_fusion
  224.8 0.0 all-gather.2.cloned.1.call-update
  224.8 38.1 %all-gather.2.cloned.1.call-done = f32[4,128,1024]{2,1,0:T(8,128)} async-done(((f32[4,16,1024]{2,1,0:T(8,128)}), f32[4,128,1024]{2,1,0:T(8,128)}) %all-gather.2.cloned.1.call-update) | async-done | bytes 2097168 | tf_op jit(solution)/shard_map/all_gather | solution.py:24
  262.9 3.4 %convolution_bitcast_fusion.1 = f32[16,128]{1,0:T(8,128)S(1)} fusion(f32[4,16,1024]{2,1,0:T(8,128)} %constant_dynamic-slice_fusion, f32[4,128,1024]{2,1,0:T(8,128)} %all-gather.2.cloned.1.call-done), kind=kOutput, calls=%fused_computation.5 | convolution fusion | flops 100663296 | bytes 2367488 | tf_op jit(solution)/shard_map/rim,rjm->ij/dot_general | solution.py:21
  266.3 38.7 %psum.15 = f32[16,128]{1,0:T(8,128)S(1)} all-reduce(f32[16,128]{1,0:T(8,128)S(1)} %convolution_bitcast_fusion.1), channel_id=1, replica_groups=mesh['wa'=16,'an'=8] {'wa'}, use_global_device_ids=true, to_apply=%region_1.0 | all-reduce | flops 2048 | bytes 16384 | tf_op jit(solution)/shard_map/psum | solution.py:27
  305.0 0.6 broadcast_multiply_fusion
Async XLA Ops:
  6.5 22.7 %copy-start = (f32[256,64]{0,1:T(8,128)S(1)}, f32[256,64]{0,1:T(8,128)}, u32[]{:S(2)}) copy-start(f32[256,64]{0,1:T(8,128)} %param.5) | copy-start | bytes 196612
  6.5 216.6 %all-reduce.2.cloned.1.call-start = ((), (), s32[]{:S(2)}) async-start(), calls=%async_computation | async-start | bytes 8388608 | tf_op jit(solution)/shard_map/psum | solution.py:19
  29.3 5.6 %copy-start.1 = (f32[16,64]{1,0:T(8,128)S(1)}, f32[16,64]{1,0:T(8,128)}, u32[]{:S(2)}) copy-start(f32[16,64]{1,0:T(8,128)} %param.6) | copy-start | bytes 12292
  64.4 198.5 %all-gather.2.cloned.1.call-start = ((), (), s32[]{:S(2)}) async-start(), calls=%async_computation.1 | async-start | bytes 2359296 | tf_op jit(solution)/shard_map/all_gather | solution.py:24
Sparse Core Ops, SparseCore 0:
  64.5 158.5 all-reduce.1
  224.9 37.9 all-gather.1
where the time goes:
time: 313 us; the launch traced here: 312 us
  waiting for transfers between devices  197 us (63%)
  matrix products  45.2 us (14%)
  blocking collectives  38.7 us (12%)
  local copies, waits for them, and re-layouts  17.6 us (6%)
  between operations  13.5 us (4%)
    psum x1, waiting for transfers between devices, on_device(): lax.psum(term.reshape(rank_one, slab_cells, rank_four * rank_two), 'wa')  159 us
    psum x1, blocking collectives, on_device(): gram_rows = lax.psum(partial_gram, 'wa')  38.7 us
    all_gather x1, waiting for transfers between devices, on_device(): lax.all_gather(owned_slab, 'an', axis=1, tiled=True)  38.1 us
    dot_general x1, matrix products, on_device(): jnp.dot(factor_four.T, mass_field.reshape(species_count, -1), precision=h...  22.7 us
    dot_general x1, matrix products, on_device(): jnp.einsum('qjkr,jp->rkqp', mixed_rows, factor_two, precision=highest)  13.5 us
    transpose x1, local copies, waits for them, and re-layouts, on_device(): jnp.einsum('qjkr,jp->rkqp', mixed_rows, factor_two, precision=highest)  8.34 us
    reshape x1, local copies, waits for them, and re-layouts, on_device(): term.reshape(rank_one, slab_cells, rank_four * rank_two)  7.61 us
  transfers between devices with their start and end apart: 2, of which 2 were waited for; matrix products, arithmetic and copies ran while one was open for 0% of the time, Pallas kernels for 0%

commit v1 on v0

--- a/solution.py
+++ b/solution.py
@@ -24,7 +24,7 @@
         lax.all_gather(owned_slab, "an", axis=1, tiled=True),
         precision=highest,
     )
-    gram_rows = lax.psum(partial_gram, "wa")
+    gram_rows = jnp.sum(lax.all_gather(partial_gram, "wa"), axis=0)
     return gram_rows / (rank_one * rank_two * rank_four)
 
 

time: 313 us -> 304 us (0.971)
  blocking collectives: 38.7 us -> 30.1 us
    psum x1 -> x0, blocking collectives: 38.7 us -> none  [on_device(): gram_rows = lax.psum(partial_gram, 'wa')]
    all_gather x0 -> x1, blocking collectives: none -> 30.1 us  [on_device(): gram_rows = jnp.sum(lax.all_gather(partial_gram, 'wa'), axis=0)]
where the time goes in v1:
time: 304 us
  waiting for transfers between devices  197 us (65%)
  matrix products  45.2 us (15%)
  blocking collectives  30.1 us (10%)
  local copies, waits for them, and re-layouts  17.6 us (6%)
  between operations  13.5 us (4%)
    psum x1, waiting for transfers between devices, on_device(): lax.psum(term.reshape(rank_one, slab_cells, rank_four * rank_two), 'wa')  159 us
    all_gather x1, waiting for transfers between devices, on_device(): lax.all_gather(owned_slab, 'an', axis=1, tiled=True)  38.1 us
    all_gather x1, blocking collectives, on_device(): gram_rows = jnp.sum(lax.all_gather(partial_gram, 'wa'), axis=0)  30.1 us
    dot_general x1, matrix products, on_device(): jnp.dot(factor_four.T, mass_field.reshape(species_count, -1), precision=h...  22.7 us
    dot_general x1, matrix products, on_device(): jnp.einsum('qjkr,jp->rkqp', mixed_rows, factor_two, precision=highest)  13.5 us
    transpose x1, local copies, waits for them, and re-layouts, on_device(): jnp.einsum('qjkr,jp->rkqp', mixed_rows, factor_two, precision=highest)  8.34 us
    reshape x1, local copies, waits for them, and re-layouts, on_device(): term.reshape(rank_one, slab_cells, rank_four * rank_two)  7.61 us
  transfers between devices with their start and end apart: 2, of which 2 were waited for; matrix products, arithmetic and copies ran while one was open for 0% of the time, Pallas kernels for 0%

profile of v1, /device:TPU:1, one launch (start us, length us, event | category | flops | bytes accessed | tf_op | source)
XLA Modules:
  0.0 303.9 jit_solution(16447354227344661514)
XLA Ops:
  6.5 0.0 copy-start
  6.5 0.0 all-reduce.2.cloned.1.call-start
  6.5 22.7 %fusion = f32[16,16,16,256]{3,0,2,1:T(8,128)S(1)} fusion(f32[16,16,256,64]{2,1,0,3:T(8,128)} %bitcast.36, f32[64,16]{0,1:T(8,128)} %param.7), kind=kOutput, calls=%fused_computation | convolution fusion | flops 805306368 | bytes 20975616 | tf_op jit(solution)/shard_map/dot_general | solution.py:13
  29.3 0.0 copy-done
  29.3 0.0 copy-start.1
  29.3 5.6 %fusion.2 = f32[16,16,16,64]{3,1,2,0:T(8,128)S(1)} fusion(f32[16,16,16,256]{3,0,2,1:T(8,128)S(1)} %fusion, f32[256,64]{0,1:T(8,128)S(1)} %copy-done), kind=kOutput, calls=%fused_computation.2 | convolution fusion | flops 805306368 | bytes 5308416 | tf_op jit(solution)/shard_map/dot_general | solution.py:16
  34.9 0.0 copy-done.1
  34.9 13.5 %convolution_bitcast_fusion = f32[64,16,16,64]{3,0,1,2:T(8,128)S(1)} fusion(f32[16,16,16,64]{3,1,2,0:T(8,128)S(1)} %fusion.2, f32[16,64]{1,0:T(8,128)S(1)} %copy-done.1), kind=kOutput, calls=%fused_computation.4 | convolution fusion | flops 201326592 | bytes 5246976 | tf_op jit(solution)/shard_map/qjkr,jp->rkqp/dot_general | solution.py:18
  48.4 8.3 %copy.5 = f32[64,16,16,64]{3,2,1,0:T(8,128)} copy(f32[64,16,16,64]{3,0,1,2:T(8,128)S(1)} %convolution_bitcast_fusion) | data formatting | bytes 8388608 | tf_op jit(solution)/shard_map/qjkr,jp->rkqp/transpose | solution.py:18
  56.7 7.6 %reshape.12 = f32[64,16,1024]{2,1,0:T(8,128)} reshape(f32[64,16,16,64]{3,2,1,0:T(8,128)} %copy.5) | data formatting | bytes 8388608 | tf_op jit(solution)/shard_map/reshape | solution.py:19
  64.3 0.0 all-reduce.2.cloned.1.call-update
  64.4 0.0 all-gather.3.cloned.1.call-start
  64.4 158.7 %all-reduce.2.cloned.1.call-done = f32[64,16,1024]{2,1,0:T(8,128)} async-done(((f32[64,16,1024]{2,1,0:T(8,128)}), f32[64,16,1024]{2,1,0:T(8,128)}) %all-reduce.2.cloned.1.call-update) | async-done | bytes 4194320 | tf_op jit(solution)/shard_map/psum | solution.py:19
  223.1 1.7 constant_dynamic-slice_fusion
  224.8 0.0 all-gather.3.cloned.1.call-update
  224.8 38.1 %all-gather.3.cloned.1.call-done = f32[4,128,1024]{2,1,0:T(8,128)} async-done(((f32[4,16,1024]{2,1,0:T(8,128)}), f32[4,128,1024]{2,1,0:T(8,128)}) %all-gather.3.cloned.1.call-update) | async-done | bytes 2097168 | tf_op jit(solution)/shard_map/all_gather | solution.py:24
  262.9 3.4 %convolution_bitcast_fusion.1 = f32[16,128]{1,0:T(8,128)S(1)} fusion(f32[4,16,1024]{2,1,0:T(8,128)} %constant_dynamic-slice_fusion, f32[4,128,1024]{2,1,0:T(8,128)} %all-gather.3.cloned.1.call-done), kind=kOutput, calls=%fused_computation.5 | convolution fusion | flops 100663296 | bytes 2367488 | tf_op jit(solution)/shard_map/rim,rjm->ij/dot_general | solution.py:21
  266.3 30.1 %all-gather = f32[256,128]{1,0:T(8,128)S(1)} all-gather(f32[16,128]{1,0:T(8,128)S(1)} %convolution_bitcast_fusion.1), channel_id=2, replica_groups=mesh['wa'=16,'an'=8] {'wa'}, dimensions={0}, use_global_device_ids=true | all-gather | bytes 139264 | tf_op jit(solution)/shard_map/all_gather | solution.py:27
  296.4 0.6 broadcast_multiply_fusion
  (1 shorter events, 0.0 us)
Async XLA Ops:
  6.5 22.7 %copy-start = (f32[256,64]{0,1:T(8,128)S(1)}, f32[256,64]{0,1:T(8,128)}, u32[]{:S(2)}) copy-start(f32[256,64]{0,1:T(8,128)} %param.5) | copy-start | bytes 196612
  6.5 216.6 %all-reduce.2.cloned.1.call-start = ((), (), s32[]{:S(2)}) async-start(), calls=%async_computation | async-start | bytes 8388608 | tf_op jit(solution)/shard_map/psum | solution.py:19
  29.3 5.6 %copy-start.1 = (f32[16,64]{1,0:T(8,128)S(1)}, f32[16,64]{1,0:T(8,128)}, u32[]{:S(2)}) copy-start(f32[16,64]{1,0:T(8,128)} %param.6) | copy-start | bytes 12292
  64.4 198.5 %all-gather.3.cloned.1.call-start = ((), (), s32[]{:S(2)}) async-start(), calls=%async_computation.1 | async-start | bytes 2359296 | tf_op jit(solution)/shard_map/all_gather | solution.py:24
Sparse Core Ops, SparseCore 0:
  64.5 158.5 all-reduce.1
  224.9 37.9 all-gather.2
